TPU v7x, 256 devices: a whole 4x4x8 slice. The times are simulated.
256 devices in a mesh: seq: 64 (over z_hi, y, x, core), tp: 4 (over z_lo).
Axes of the slice: x: 4, y: 4, z: 8 (z_hi: 2, z_lo: 4; z = z_hi * 4 + z_lo), core: 2. Of those that a mesh axis runs over, the one named last changes fastest.
Arguments:
- residual: bfloat16 [32768, 2048], P('seq', 'tp'), may hold values from -6 to 6
- norm_gain: float32 [2048], replicated, may hold values from 0.3 to 3
- query_weight: bfloat16 [2048, 1024], P(None, 'tp'), as said below
- key_weight: bfloat16 [2048, 1024], P(None, 'tp'), as said below
- value_weight: bfloat16 [2048, 1024], P(None, 'tp'), may hold values from -0.375 to 0.375
- out_weight: bfloat16 [1024, 2048], P('tp'), may hold values from -0.1875 to 0.1875
- segment_start: int32 [32768], P('seq'), may hold values from 0 to 32640, as said below
- token_valid: int32 [32768], P('seq'), may hold values from 0 to 1, as said below
- page_slot: int32 [256], P('seq'), may hold values from 4 to 511, as said below
Outputs:
- hidden: bfloat16 [32768, 2048], P('seq', 'tp')
- cache: bfloat16 [512, 128, 2048], P('seq', None, 'tp')
Inputs may be any that keep to these rules, and one draw needn't show every extreme that they name: `segment_start`: prompts start at multiples of 128 and are contiguous; each holds at most 8192 tokens and one holds exactly 8192. `token_valid`: zeros form a tail of the last page of a prompt; the first token of every prompt is 1. No two pages share a cache page; page_slot // 8 is the device that holds the page's tokens, or the next device when that one holds tokens of the same prompt. `query_weight`: independent entries whose scale falls as the inverse square root of 2048. `key_weight`: independent entries whose scale falls as the inverse square root of 2048.
All inputs are finite; a program needn't handle non-finite values.
Results may differ from a plain program's by a relative error of at most 0.02.
The roundings to bfloat16 on the way count: a program that leaves them out, or rounds other values in their place, can miss the bound.
Values may be sent and summed in bfloat16 or wider, within the bound.
No kernel may reach another device: no remote copies, remote signals or barrier semaphores. Data moves between devices by JAX's collectives and lax.ppermute only.
A program may use at most 128 MiB of HBM per device.

v0:
```python
import jax
import jax.numpy as jnp
from jax import lax
from jax.sharding import PartitionSpec as P

HD = 64
PAGE = 128
SPAN = 16
THETA = 130000.0
EPS = 1e-05


def passed_along(x, axis, by):
    count = lax.axis_size(axis)
    pairs = [(i, i + by) for i in range(count) if 0 <= i + by < count]
    return lax.ppermute(x, axis, pairs)


def rotate(inputs, positions):
    half_dim = inputs.shape[-1] // 2
    frequency = THETA ** (-2.0 * jnp.arange(half_dim, dtype=jnp.float32) / inputs.shape[-1])
    angles = positions.astype(jnp.float32)[:, None] * frequency[None, :]
    cosine = jnp.cos(angles)[:, None, :]
    sine_part = jnp.sin(angles)[:, None, :]
    front_half = inputs[..., :half_dim]
    back_half = inputs[..., half_dim:]
    return jnp.concatenate(
        [front_half * cosine - back_half * sine_part, back_half * cosine + front_half * sine_part],
        axis=-1,
    )


def body(
    residual,
    norm_gain,
    query_weight,
    key_weight,
    value_weight,
    out_weight,
    segment_start,
    token_valid,
    page_slot,
):
    row_count = residual.shape[0]
    local_heads = query_weight.shape[1] // HD
    gathered = lax.all_gather(residual, "tp", axis=1, tiled=True)
    widened = gathered.astype(jnp.float32)
    mean_sq = jnp.mean(widened * widened, axis=1, keepdims=True)
    normed = (widened * lax.rsqrt(mean_sq + EPS) * norm_gain[None, :]).astype(jnp.bfloat16)
    seq_rank = lax.axis_index("seq")
    first_row = seq_rank * row_count
    places = first_row + jnp.arange(row_count, dtype=jnp.int32)
    offsets = places - segment_start
    queries = jnp.dot(normed, query_weight, preferred_element_type=jnp.float32).reshape(
        row_count, local_heads, HD
    )
    queries = rotate(queries, offsets).astype(jnp.bfloat16)
    key_rot = jnp.dot(normed, key_weight, preferred_element_type=jnp.float32).reshape(
        row_count, local_heads, HD
    )
    key_rot = rotate(key_rot, offsets).astype(jnp.bfloat16)
    values = (
        jnp.dot(normed, value_weight, preferred_element_type=jnp.float32)
        .reshape(row_count, local_heads, HD)
        .astype(jnp.bfloat16)
    )
    packed = jnp.concatenate([key_rot[:, :, None, :], values[:, :, None, :]], axis=2).reshape(
        row_count, local_heads * 2 * HD
    )
    packed = jnp.where(token_valid[:, None] > 0, packed, jnp.zeros_like(packed))
    key_group = jnp.where(token_valid > 0, segment_start, -1)
    in_page = jnp.arange(row_count, dtype=jnp.int32) % PAGE
    page_rows = jnp.repeat(page_slot, PAGE) * PAGE + in_page
    slot_count = 2 * page_slot.shape[0]
    cache_size = slot_count * PAGE
    base_row = seq_rank * cache_size
    score_scale = HD ** (-0.5)

    def attend_block(running, incoming, allowed):
        row_max, norm_sum, weighted = running
        key_value = incoming[0].reshape(incoming[0].shape[0], local_heads, 2, HD)
        scores = (
            jnp.einsum(
                "qhd,khd->hqk", queries, key_value[:, :, 0, :], preferred_element_type=jnp.float32
            )
            * score_scale
        )
        block_max = jnp.max(jnp.where(allowed[None], scores, -1e30), axis=2)
        new_max = jnp.maximum(row_max, block_max)
        weights = jnp.where(allowed[None], jnp.exp(scores - new_max[:, :, None]), 0.0)
        shrink = jnp.exp(row_max - new_max)
        norm_sum = norm_sum * shrink + jnp.sum(weights, axis=2)
        update = jnp.einsum(
            "hqk,khd->qhd",
            weights.astype(jnp.bfloat16),
            key_value[:, :, 1, :],
            preferred_element_type=jnp.float32,
        )
        weighted = weighted * jnp.transpose(shrink)[:, :, None] + update
        return (new_max, norm_sum, weighted)

    def absorb(carried, incoming, begin_row):
        row_max, norm_sum, weighted, cache_rows = carried
        key_count = incoming[0].shape[0]
        key_places = begin_row + jnp.arange(key_count, dtype=jnp.int32)
        allowed = (
            (incoming[1][None, :] == segment_start[:, None])
            & (key_places[None, :] <= places[:, None])
            & (key_places[None, :] >= 0)
        )
        local_dest = incoming[2] - base_row
        in_range = (local_dest >= 0) & (local_dest < cache_size) & (key_places >= 0)
        target = jnp.where(in_range, local_dest, cache_size)
        cache_rows = cache_rows.at[target].set(incoming[0], mode="drop")
        running = attend_block((row_max, norm_sum, weighted), incoming, allowed)
        return (running[0], running[1], running[2], cache_rows)

    initial = (
        jnp.full((local_heads, row_count), -1e30, jnp.float32),
        jnp.zeros((local_heads, row_count), jnp.float32),
        jnp.zeros((row_count, local_heads, HD), jnp.float32),
        jnp.zeros((cache_size, local_heads * 2 * HD), jnp.bfloat16),
    )
    own_block = (packed, key_group, page_rows)
    carried = absorb(initial, own_block, first_row)
    reach_dev = min(SPAN, lax.axis_size("seq") // 2)

    def advance(step_index, carry_in):
        moving, carry_state = carry_in
        moving = passed_along((moving[0], moving[1], moving[2]), "seq", 1)
        carry_state = absorb(carry_state, moving, first_row - (step_index + 1) * row_count)
        return (moving, carry_state)

    moving, carried = lax.fori_loop(0, reach_dev, advance, (own_block, carried))
    row_max, norm_sum, weighted, cache_rows = carried
    attended = (
        (weighted / jnp.transpose(norm_sum)[:, :, None])
        .astype(jnp.bfloat16)
        .reshape(row_count, local_heads * HD)
    )
    projected = jnp.dot(attended, out_weight, preferred_element_type=jnp.float32)
    summed = lax.psum_scatter(
        projected.astype(jnp.bfloat16), "tp", scatter_dimension=1, tiled=True
    ).astype(jnp.float32)
    hidden = (residual.astype(jnp.float32) + summed).astype(jnp.bfloat16)
    return (hidden, cache_rows.reshape(slot_count, PAGE, local_heads * 2 * HD))


def solution(mesh):
    return jax.shard_map(
        body,
        mesh=mesh,
        in_specs=(
            P("seq", "tp"),
            P(),
            P(None, "tp"),
            P(None, "tp"),
            P(None, "tp"),
            P("tp", None),
            P("seq"),
            P("seq"),
            P("seq"),
        ),
        out_specs=(P("seq", "tp"), P("seq", None, "tp")),
        check_vma=False,
    )
```

profile of v0, /device:TPU:1, one launch (start us, length us, event | category | flops | bytes accessed | tf_op | source)
XLA Modules:
  0.0 631.6 jit_solution(17440001359176810723)
XLA Ops:
  10.9 52.2 %all-gather.2.cloned.1.call-done = bf16[512,2048]{1,0:T(8,128)(2,1)} async-done(((bf16[512,512]{1,0:T(8,128)(2,1)}), bf16[512,2048]{1,0:T(8,128)(2,1)}) %all-gather.2.cloned.1.call-update) | async-done | bytes 2097168 | tf_op jit(solution)/shard_map/all_gather | solution.py:46
  77.5 398.4 %while.27 = (s32[]{:T(128)}, bf16[512,512]{0,1:T(8,128)(2,1)S(1)}, s32[512]{0:T(512)S(1)}, s32[512]{0:T(512)S(1)}, f32[4,512]{1,0:T(4,128)S(1)}, /*index=5*/f32[...) while((s32[]{:T(128)}, bf16[512,512]{0,1:T(8,128)(2,1)S(1)}, ...), condition=%wide.region_8.9_spmd.clone.clone, body=%wide.region_4.8_spmd.clone.clone.sunk | while | flops 281293824 | bytes 21409060 | solution.py:134
  87.5 5.7 collective-permute-done
  101.2 4.4 collective-permute-start.2
  111.2 5.7 collective-permute-done
  124.9 4.4 collective-permute-start.2
  135.1 5.7 collective-permute-done
  156.4 4.4 collective-permute-start
  161.2 5.7 collective-permute-done
  185.7 5.7 collective-permute-done
  210.1 5.7 collective-permute-done
  234.6 5.7 collective-permute-done
  259.1 5.7 collective-permute-done
  283.6 5.7 collective-permute-done
  308.1 5.7 collective-permute-done
  332.6 5.7 collective-permute-done
  357.1 5.7 collective-permute-done
  381.6 5.7 collective-permute-done
  406.1 5.7 collective-permute-done
  430.5 5.7 collective-permute-done
  448.7 8.7 %collective-permute-start.1 = (s32[512]{0:T(512)S(1)}, s32[512]{0:T(512)S(1)}, u32[]{:S(2)}, u32[]{:S(2)}) collective-permute-start(s32[512]{0:T(512)S(1)} %get-tuple-element.427), channel_id=1, source_target_pairs={{0,4},{4,8},{8,12},{12,16},{16,20},{20,24},{24,28},{28,32},{32,36}... | collective-permute-start | bytes 6152 | tf_op jit(solution)/shard_map/while/body/eval_jaxpr/ppermute | solution.py:16
  457.4 4.4 collective-permute-start
  462.2 5.7 collective-permute-done
  479.5 143.3 %reduce-scatter.2.cloned.1.call-done = bf16[512,512]{1,0:T(8,128)(2,1)} async-done(((bf16[512,2048]{1,0:T(8,128)(2,1)}), bf16[512,512]{1,0:T(8,128)(2,1)}) %reduce-scatter.2.cloned.1.call-update) | async-done | bytes 524304 | tf_op jit(solution)/shard_map/reduce_scatter | solution.py:142
  (364 shorter events, 302.0 us)
Async XLA Ops:
  7.2 55.9 %all-gather.2.cloned.1.call-start = ((), (), s32[]{:S(2)}) async-start(), calls=%async_computation.1 | async-start | bytes 2621440 | tf_op jit(solution)/shard_map/all_gather | solution.py:46
  7.9 614.9 %reduce-scatter.2.cloned.1.call-start = ((), (), s32[]{:S(2)}) async-start(), calls=%async_computation.2 | async-start | bytes 2621440 | tf_op jit(solution)/shard_map/reduce_scatter | solution.py:142
  148.8 12.0 %collective-permute-start.2 = (s32[512]{0:T(512)S(1)}, s32[512]{0:T(512)S(1)}, u32[]{:S(2)}, u32[]{:S(2)}) collective-permute-start(s32[512]{0:T(512)S(1)} %get-tuple-element.428), channel_id=1, source_target_pairs={{0,4},{4,8},{8,12},{12,16},{16,20},{20,24},{24,28},{28,32},{32,36}... | collective-permute-start | bytes 6152 | tf_op jit(solution)/shard_map/while/body/eval_jaxpr/ppermute | solution.py:16
  156.4 10.5 %collective-permute-start = (bf16[512,512]{0,1:T(8,128)(2,1)S(1)}, bf16[512,512]{0,1:T(8,128)(2,1)S(1)}, u32[]{:S(2)}, u32[]{:S(2)}) collective-permute-start(bf16[512,512]{0,1:T(8,128)(2,1)S(1)} %get-tuple-element.426), channel_id=1, source_target_pairs={{0,4},{4,8},{8,12},{12,16},{16,20},{20,24},{24,28},{28,32},{32,36}... | collective-permute-start | bytes 1572872 | tf_op jit(solution)/shard_map/while/body/eval_jaxpr/ppermute | solution.py:16
  174.9 10.4 %collective-permute-start.2 = (s32[512]{0:T(512)S(1)}, s32[512]{0:T(512)S(1)}, u32[]{:S(2)}, u32[]{:S(2)}) collective-permute-start(s32[512]{0:T(512)S(1)} %get-tuple-element.428), channel_id=1, source_target_pairs={{0,4},{4,8},{8,12},{12,16},{16,20},{20,24},{24,28},{28,32},{32,36}... | collective-permute-start | bytes 6152 | tf_op jit(solution)/shard_map/while/body/eval_jaxpr/ppermute | solution.py:16
  181.2 10.1 %collective-permute-start = (bf16[512,512]{0,1:T(8,128)(2,1)S(1)}, bf16[512,512]{0,1:T(8,128)(2,1)S(1)}, u32[]{:S(2)}, u32[]{:S(2)}) collective-permute-start(bf16[512,512]{0,1:T(8,128)(2,1)S(1)} %get-tuple-element.426), channel_id=1, source_target_pairs={{0,4},{4,8},{8,12},{12,16},{16,20},{20,24},{24,28},{28,32},{32,36}... | collective-permute-start | bytes 1572872 | tf_op jit(solution)/shard_map/while/body/eval_jaxpr/ppermute | solution.py:16
  199.4 10.4 %collective-permute-start.2 = (s32[512]{0:T(512)S(1)}, s32[512]{0:T(512)S(1)}, u32[]{:S(2)}, u32[]{:S(2)}) collective-permute-start(s32[512]{0:T(512)S(1)} %get-tuple-element.428), channel_id=1, source_target_pairs={{0,4},{4,8},{8,12},{12,16},{16,20},{20,24},{24,28},{28,32},{32,36}... | collective-permute-start | bytes 6152 | tf_op jit(solution)/shard_map/while/body/eval_jaxpr/ppermute | solution.py:16
  205.7 10.1 %collective-permute-start = (bf16[512,512]{0,1:T(8,128)(2,1)S(1)}, bf16[512,512]{0,1:T(8,128)(2,1)S(1)}, u32[]{:S(2)}, u32[]{:S(2)}) collective-permute-start(bf16[512,512]{0,1:T(8,128)(2,1)S(1)} %get-tuple-element.426), channel_id=1, source_target_pairs={{0,4},{4,8},{8,12},{12,16},{16,20},{20,24},{24,28},{28,32},{32,36}... | collective-permute-start | bytes 1572872 | tf_op jit(solution)/shard_map/while/body/eval_jaxpr/ppermute | solution.py:16
  223.9 10.4 %collective-permute-start.2 = (s32[512]{0:T(512)S(1)}, s32[512]{0:T(512)S(1)}, u32[]{:S(2)}, u32[]{:S(2)}) collective-permute-start(s32[512]{0:T(512)S(1)} %get-tuple-element.428), channel_id=1, source_target_pairs={{0,4},{4,8},{8,12},{12,16},{16,20},{20,24},{24,28},{28,32},{32,36}... | collective-permute-start | bytes 6152 | tf_op jit(solution)/shard_map/while/body/eval_jaxpr/ppermute | solution.py:16
  230.2 10.1 %collective-permute-start = (bf16[512,512]{0,1:T(8,128)(2,1)S(1)}, bf16[512,512]{0,1:T(8,128)(2,1)S(1)}, u32[]{:S(2)}, u32[]{:S(2)}) collective-permute-start(bf16[512,512]{0,1:T(8,128)(2,1)S(1)} %get-tuple-element.426), channel_id=1, source_target_pairs={{0,4},{4,8},{8,12},{12,16},{16,20},{20,24},{24,28},{28,32},{32,36}... | collective-permute-start | bytes 1572872 | tf_op jit(solution)/shard_map/while/body/eval_jaxpr/ppermute | solution.py:16
  248.4 10.4 %collective-permute-start.2 = (s32[512]{0:T(512)S(1)}, s32[512]{0:T(512)S(1)}, u32[]{:S(2)}, u32[]{:S(2)}) collective-permute-start(s32[512]{0:T(512)S(1)} %get-tuple-element.428), channel_id=1, source_target_pairs={{0,4},{4,8},{8,12},{12,16},{16,20},{20,24},{24,28},{28,32},{32,36}... | collective-permute-start | bytes 6152 | tf_op jit(solution)/shard_map/while/body/eval_jaxpr/ppermute | solution.py:16
  254.7 10.1 %collective-permute-start = (bf16[512,512]{0,1:T(8,128)(2,1)S(1)}, bf16[512,512]{0,1:T(8,128)(2,1)S(1)}, u32[]{:S(2)}, u32[]{:S(2)}) collective-permute-start(bf16[512,512]{0,1:T(8,128)(2,1)S(1)} %get-tuple-element.426), channel_id=1, source_target_pairs={{0,4},{4,8},{8,12},{12,16},{16,20},{20,24},{24,28},{28,32},{32,36}... | collective-permute-start | bytes 1572872 | tf_op jit(solution)/shard_map/while/body/eval_jaxpr/ppermute | solution.py:16
  272.8 10.4 %collective-permute-start.2 = (s32[512]{0:T(512)S(1)}, s32[512]{0:T(512)S(1)}, u32[]{:S(2)}, u32[]{:S(2)}) collective-permute-start(s32[512]{0:T(512)S(1)} %get-tuple-element.428), channel_id=1, source_target_pairs={{0,4},{4,8},{8,12},{12,16},{16,20},{20,24},{24,28},{28,32},{32,36}... | collective-permute-start | bytes 6152 | tf_op jit(solution)/shard_map/while/body/eval_jaxpr/ppermute | solution.py:16
  279.2 10.1 %collective-permute-start = (bf16[512,512]{0,1:T(8,128)(2,1)S(1)}, bf16[512,512]{0,1:T(8,128)(2,1)S(1)}, u32[]{:S(2)}, u32[]{:S(2)}) collective-permute-start(bf16[512,512]{0,1:T(8,128)(2,1)S(1)} %get-tuple-element.426), channel_id=1, source_target_pairs={{0,4},{4,8},{8,12},{12,16},{16,20},{20,24},{24,28},{28,32},{32,36}... | collective-permute-start | bytes 1572872 | tf_op jit(solution)/shard_map/while/body/eval_jaxpr/ppermute | solution.py:16
  297.3 10.4 %collective-permute-start.2 = (s32[512]{0:T(512)S(1)}, s32[512]{0:T(512)S(1)}, u32[]{:S(2)}, u32[]{:S(2)}) collective-permute-start(s32[512]{0:T(512)S(1)} %get-tuple-element.428), channel_id=1, source_target_pairs={{0,4},{4,8},{8,12},{12,16},{16,20},{20,24},{24,28},{28,32},{32,36}... | collective-permute-start | bytes 6152 | tf_op jit(solution)/shard_map/while/body/eval_jaxpr/ppermute | solution.py:16
  303.7 10.1 %collective-permute-start = (bf16[512,512]{0,1:T(8,128)(2,1)S(1)}, bf16[512,512]{0,1:T(8,128)(2,1)S(1)}, u32[]{:S(2)}, u32[]{:S(2)}) collective-permute-start(bf16[512,512]{0,1:T(8,128)(2,1)S(1)} %get-tuple-element.426), channel_id=1, source_target_pairs={{0,4},{4,8},{8,12},{12,16},{16,20},{20,24},{24,28},{28,32},{32,36}... | collective-permute-start | bytes 1572872 | tf_op jit(solution)/shard_map/while/body/eval_jaxpr/ppermute | solution.py:16
  321.8 10.4 %collective-permute-start.2 = (s32[512]{0:T(512)S(1)}, s32[512]{0:T(512)S(1)}, u32[]{:S(2)}, u32[]{:S(2)}) collective-permute-start(s32[512]{0:T(512)S(1)} %get-tuple-element.428), channel_id=1, source_target_pairs={{0,4},{4,8},{8,12},{12,16},{16,20},{20,24},{24,28},{28,32},{32,36}... | collective-permute-start | bytes 6152 | tf_op jit(solution)/shard_map/while/body/eval_jaxpr/ppermute | solution.py:16
  346.3 10.4 %collective-permute-start.2 = (s32[512]{0:T(512)S(1)}, s32[512]{0:T(512)S(1)}, u32[]{:S(2)}, u32[]{:S(2)}) collective-permute-start(s32[512]{0:T(512)S(1)} %get-tuple-element.428), channel_id=1, source_target_pairs={{0,4},{4,8},{8,12},{12,16},{16,20},{20,24},{24,28},{28,32},{32,36}... | collective-permute-start | bytes 6152 | tf_op jit(solution)/shard_map/while/body/eval_jaxpr/ppermute | solution.py:16
  370.8 10.4 %collective-permute-start.2 = (s32[512]{0:T(512)S(1)}, s32[512]{0:T(512)S(1)}, u32[]{:S(2)}, u32[]{:S(2)}) collective-permute-start(s32[512]{0:T(512)S(1)} %get-tuple-element.428), channel_id=1, source_target_pairs={{0,4},{4,8},{8,12},{12,16},{16,20},{20,24},{24,28},{28,32},{32,36}... | collective-permute-start | bytes 6152 | tf_op jit(solution)/shard_map/while/body/eval_jaxpr/ppermute | solution.py:16
  395.3 10.4 %collective-permute-start.2 = (s32[512]{0:T(512)S(1)}, s32[512]{0:T(512)S(1)}, u32[]{:S(2)}, u32[]{:S(2)}) collective-permute-start(s32[512]{0:T(512)S(1)} %get-tuple-element.428), channel_id=1, source_target_pairs={{0,4},{4,8},{8,12},{12,16},{16,20},{20,24},{24,28},{28,32},{32,36}... | collective-permute-start | bytes 6152 | tf_op jit(solution)/shard_map/while/body/eval_jaxpr/ppermute | solution.py:16
  419.8 10.4 %collective-permute-start.2 = (s32[512]{0:T(512)S(1)}, s32[512]{0:T(512)S(1)}, u32[]{:S(2)}, u32[]{:S(2)}) collective-permute-start(s32[512]{0:T(512)S(1)} %get-tuple-element.428), channel_id=1, source_target_pairs={{0,4},{4,8},{8,12},{12,16},{16,20},{20,24},{24,28},{28,32},{32,36}... | collective-permute-start | bytes 6152 | tf_op jit(solution)/shard_map/while/body/eval_jaxpr/ppermute | solution.py:16
  444.3 17.6 %collective-permute-start.2 = (s32[512]{0:T(512)S(1)}, s32[512]{0:T(512)S(1)}, u32[]{:S(2)}, u32[]{:S(2)}) collective-permute-start(s32[512]{0:T(512)S(1)} %get-tuple-element.428), channel_id=1, source_target_pairs={{0,4},{4,8},{8,12},{12,16},{16,20},{20,24},{24,28},{28,32},{32,36}... | collective-permute-start | bytes 6152 | tf_op jit(solution)/shard_map/while/body/eval_jaxpr/ppermute | solution.py:16
  448.7 13.2 %collective-permute-start.1 = (s32[512]{0:T(512)S(1)}, s32[512]{0:T(512)S(1)}, u32[]{:S(2)}, u32[]{:S(2)}) collective-permute-start(s32[512]{0:T(512)S(1)} %get-tuple-element.427), channel_id=1, source_target_pairs={{0,4},{4,8},{8,12},{12,16},{16,20},{20,24},{24,28},{28,32},{32,36}... | collective-permute-start | bytes 6152 | tf_op jit(solution)/shard_map/while/body/eval_jaxpr/ppermute | solution.py:16
  457.4 10.5 %collective-permute-start = (bf16[512,512]{0,1:T(8,128)(2,1)S(1)}, bf16[512,512]{0,1:T(8,128)(2,1)S(1)}, u32[]{:S(2)}, u32[]{:S(2)}) collective-permute-start(bf16[512,512]{0,1:T(8,128)(2,1)S(1)} %get-tuple-element.426), channel_id=1, source_target_pairs={{0,4},{4,8},{8,12},{12,16},{16,20},{20,24},{24,28},{28,32},{32,36}... | collective-permute-start | bytes 1572872 | tf_op jit(solution)/shard_map/while/body/eval_jaxpr/ppermute | solution.py:16
  (34 other events, 1097.3 us)
Sparse Core Ops, SparseCore 0:
  9.8 53.2 all-gather.1
  479.7 143.1 reduce-scatter.1
where the time goes:
time: 634 us; the launch traced here: 632 us
  waiting for transfers between devices  287 us (45%)
  starting transfers between devices  172 us (27%)
  matrix products  70.6 us (11%)
  local copies, waits for them, and re-layouts  54.7 us (9%)
  other arithmetic  30.1 us (5%)
  between operations  14.3 us (2%)
    ppermute x48, starting transfers between devices, passed_along(): return lax.ppermute(x, axis, pairs)  172 us
    reduce_scatter x1, waiting for transfers between devices, body(): lax.psum_scatter(projected.astype(jnp.bfloat16), 'tp', scatter_dimension=...  143 us
    ppermute x48, waiting for transfers between devices, passed_along(): return lax.ppermute(x, axis, pairs)  91.2 us
    all_gather x1, waiting for transfers between devices, body(): gathered = lax.all_gather(residual, 'tp', axis=1, tiled=True)  52.2 us
    scatter x17, local copies, waits for them, and re-layouts, absorb(): cache_rows = cache_rows.at[target].set(incoming[0], mode='drop')  50.2 us
    dot_general x17, matrix products, attend_block(): jnp.einsum('hqk,khd->qhd', weights.astype(jnp.bfloat16), key_value[:, :,...  48.4 us
    reduce_sum x17, other arithmetic, attend_block(): norm_sum = norm_sum * shrink + jnp.sum(weights, axis=2)  15.5 us
    dot_general x17, matrix products, attend_block(): jnp.einsum('qhd,khd->hqk', queries, key_value[:, :, 0, :], preferred_elem...  15.4 us
  transfers between devices with their start and end apart: 50, of which 18 were waited for; matrix products, arithmetic and copies ran while one was open for 1% of the time, Pallas kernels for 0%

commit v1 on v0

--- a/solution.py
+++ b/solution.py
@@ -43,7 +43,9 @@
 ):
     row_count = residual.shape[0]
     local_heads = query_weight.shape[1] // HD
-    gathered = lax.all_gather(residual, "tp", axis=1, tiled=True)
+    gathered = jnp.concatenate(
+        lax.all_to_all(jnp.stack([residual] * lax.axis_size("tp")), "tp", 0, 0), axis=1
+    )
     widened = gathered.astype(jnp.float32)
     mean_sq = jnp.mean(widened * widened, axis=1, keepdims=True)
     normed = (widened * lax.rsqrt(mean_sq + EPS) * norm_gain[None, :]).astype(jnp.bfloat16)

time: 634 us -> 636 us (level)
  waiting for transfers between devices: 287 us -> 274 us
  local copies, waits for them, and re-layouts: 54.7 us -> 66 us
  starting transfers between devices: 172 us -> 181 us
    all_gather x1 -> x0, waiting for transfers between devices: 52.2 us -> none  [body(): gathered = lax.all_gather(residual, 'tp', axis=1, tiled=True)]
    all_to_all x0 -> x1, waiting for transfers between devices: none -> 41.1 us  [body(): lax.all_to_all(jnp.stack([residual] * lax.axis_size('tp')), 'tp', 0, 0)]
    all_to_all x0 -> x1, starting transfers between devices: none -> 6.43 us  [body(): lax.all_to_all(jnp.stack([residual] * lax.axis_size('tp')), 'tp', 0, 0)]
  transfers between devices with their start and end apart: 50 -> 50, of which waited for: 18 -> 18; matrix products, arithmetic and copies ran while one was open for 1% -> 2% of each run, Pallas kernels for 0% -> 0%
where the time goes in v1:
time: 636 us; the launch traced here: 633 us
  waiting for transfers between devices  274 us (43%)
  starting transfers between devices  181 us (28%)
  matrix products  68 us (11%)
  local copies, waits for them, and re-layouts  66 us (10%)
  other arithmetic  27.6 us (4%)
  between operations  14.3 us (2%)
    ppermute x48, starting transfers between devices, passed_along(): return lax.ppermute(x, axis, pairs)  174 us
    reduce_scatter x1, waiting for transfers between devices, body(): lax.psum_scatter(projected.astype(jnp.bfloat16), 'tp', scatter_dimension=...  142 us
    ppermute x48, waiting for transfers between devices, passed_along(): return lax.ppermute(x, axis, pairs)  91.2 us
    scatter x17, local copies, waits for them, and re-layouts, absorb(): cache_rows = cache_rows.at[target].set(incoming[0], mode='drop')  50.2 us
    dot_general x17, matrix products, attend_block(): jnp.einsum('hqk,khd->qhd', weights.astype(jnp.bfloat16), key_value[:, :,...  48.4 us
    all_to_all x1, waiting for transfers between devices, body(): lax.all_to_all(jnp.stack([residual] * lax.axis_size('tp')), 'tp', 0, 0)  41.1 us
    reduce_sum x17, other arithmetic, attend_block(): norm_sum = norm_sum * shrink + jnp.sum(weights, axis=2)  15.5 us
    dot_general x17, matrix products, attend_block(): jnp.einsum('qhd,khd->hqk', queries, key_value[:, :, 0, :], preferred_elem...  15.4 us
  transfers between devices with their start and end apart: 50, of which 18 were waited for; matrix products, arithmetic and copies ran while one was open for 2% of the time, Pallas kernels for 0%

profile of v1, /device:TPU:1, one launch (start us, length us, event | category | flops | bytes accessed | tf_op | source)
XLA Modules:
  0.0 633.0 jit_solution(5073541296367181563)
XLA Ops:
  9.9 6.4 %all-to-all-start = ((bf16[4,512,512]{2,1,0:T(8,128)(2,1)}), bf16[4,512,512]{2,1,0:T(8,128)(2,1)}, u32[]{:S(2)}, u32[]{:S(2)}) async-start(bf16[4,512,512]{2,1,0:T(8,128)(2,1)} %stack.2), calls=%async_computation | async-start | bytes 4194304 | tf_op jit(solution)/shard_map/all_to_all | solution.py:47
  23.1 41.1 %all-to-all-done = bf16[4,512,512]{2,1,0:T(8,128)(2,1)} async-done(((bf16[4,512,512]{2,1,0:T(8,128)(2,1)}), bf16[4,512,512]{2,1,0:T(8,128)(2,1)}, u32[]{:S(2)}, u32[]{:S(2)}) %all-to-all-start) | async-done | bytes 2097184 | tf_op jit(solution)/shard_map/all_to_all | solution.py:47
  78.3 400.6 %while.27 = (s32[]{:T(128)}, bf16[512,512]{0,1:T(8,128)(2,1)S(1)}, s32[512]{0:T(512)S(1)}, s32[512]{0:T(512)S(1)}, f32[4,512]{1,0:T(4,128)S(1)}, /*index=5*/f32[...) while((s32[]{:T(128)}, bf16[512,512]{0,1:T(8,128)(2,1)S(1)}, ...), condition=%wide.region_8.9_spmd.clone.clone, body=%wide.region_4.8_spmd.clone.clone.sunk | while | flops 281293824 | bytes 21409060 | solution.py:136
  78.3 4.4 collective-permute-start.2
  88.5 5.7 collective-permute-done
  102.3 4.4 collective-permute-start.2
  112.2 5.7 collective-permute-done
  136.2 5.7 collective-permute-done
  162.2 5.7 collective-permute-done
  186.7 5.7 collective-permute-done
  211.2 5.7 collective-permute-done
  235.7 5.7 collective-permute-done
  260.2 5.7 collective-permute-done
  284.7 5.7 collective-permute-done
  309.2 5.7 collective-permute-done
  333.7 5.7 collective-permute-done
  358.2 5.7 collective-permute-done
  382.6 5.7 collective-permute-done
  407.1 5.7 collective-permute-done
  428.4 4.4 collective-permute-start
  433.2 5.7 collective-permute-done
  451.3 9.0 %collective-permute-start.1 = (s32[512]{0:T(512)S(1)}, s32[512]{0:T(512)S(1)}, u32[]{:S(2)}, u32[]{:S(2)}) collective-permute-start(s32[512]{0:T(512)S(1)} %get-tuple-element.427), channel_id=1, source_target_pairs={{0,4},{4,8},{8,12},{12,16},{16,20},{20,24},{24,28},{28,32},{32,36}... | collective-permute-start | bytes 6152 | tf_op jit(solution)/shard_map/while/body/eval_jaxpr/ppermute | solution.py:16
  465.1 5.7 collective-permute-done
  482.5 141.7 %reduce-scatter.2.cloned.1.call-done = bf16[512,512]{1,0:T(8,128)(2,1)} async-done(((bf16[512,2048]{1,0:T(8,128)(2,1)}), bf16[512,512]{1,0:T(8,128)(2,1)}) %reduce-scatter.2.cloned.1.call-update) | async-done | bytes 524304 | tf_op jit(solution)/shard_map/reduce_scatter | solution.py:144
  (380 shorter events, 313.7 us)
Async XLA Ops:
  9.9 54.3 %all-to-all-start = ((bf16[4,512,512]{2,1,0:T(8,128)(2,1)}), bf16[4,512,512]{2,1,0:T(8,128)(2,1)}, u32[]{:S(2)}, u32[]{:S(2)}) async-start(bf16[4,512,512]{2,1,0:T(8,128)(2,1)} %stack.2), calls=%async_computation | async-start | bytes 4194304 | tf_op jit(solution)/shard_map/all_to_all | solution.py:47
  16.3 607.9 %reduce-scatter.2.cloned.1.call-start = ((), (), s32[]{:S(2)}) async-start(), calls=%async_computation.2 | async-start | bytes 2621440 | tf_op jit(solution)/shard_map/reduce_scatter | solution.py:144
  149.9 12.0 %collective-permute-start.2 = (s32[512]{0:T(512)S(1)}, s32[512]{0:T(512)S(1)}, u32[]{:S(2)}, u32[]{:S(2)}) collective-permute-start(s32[512]{0:T(512)S(1)} %get-tuple-element.428), channel_id=1, source_target_pairs={{0,4},{4,8},{8,12},{12,16},{16,20},{20,24},{24,28},{28,32},{32,36}... | collective-permute-start | bytes 6152 | tf_op jit(solution)/shard_map/while/body/eval_jaxpr/ppermute | solution.py:16
  157.4 10.5 %collective-permute-start = (bf16[512,512]{0,1:T(8,128)(2,1)S(1)}, bf16[512,512]{0,1:T(8,128)(2,1)S(1)}, u32[]{:S(2)}, u32[]{:S(2)}) collective-permute-start(bf16[512,512]{0,1:T(8,128)(2,1)S(1)} %get-tuple-element.426), channel_id=1, source_target_pairs={{0,4},{4,8},{8,12},{12,16},{16,20},{20,24},{24,28},{28,32},{32,36}... | collective-permute-start | bytes 1572872 | tf_op jit(solution)/shard_map/while/body/eval_jaxpr/ppermute | solution.py:16
  176.0 10.4 %collective-permute-start.2 = (s32[512]{0:T(512)S(1)}, s32[512]{0:T(512)S(1)}, u32[]{:S(2)}, u32[]{:S(2)}) collective-permute-start(s32[512]{0:T(512)S(1)} %get-tuple-element.428), channel_id=1, source_target_pairs={{0,4},{4,8},{8,12},{12,16},{16,20},{20,24},{24,28},{28,32},{32,36}... | collective-permute-start | bytes 6152 | tf_op jit(solution)/shard_map/while/body/eval_jaxpr/ppermute | solution.py:16
  200.5 10.4 %collective-permute-start.2 = (s32[512]{0:T(512)S(1)}, s32[512]{0:T(512)S(1)}, u32[]{:S(2)}, u32[]{:S(2)}) collective-permute-start(s32[512]{0:T(512)S(1)} %get-tuple-element.428), channel_id=1, source_target_pairs={{0,4},{4,8},{8,12},{12,16},{16,20},{20,24},{24,28},{28,32},{32,36}... | collective-permute-start | bytes 6152 | tf_op jit(solution)/shard_map/while/body/eval_jaxpr/ppermute | solution.py:16
  224.9 10.4 %collective-permute-start.2 = (s32[512]{0:T(512)S(1)}, s32[512]{0:T(512)S(1)}, u32[]{:S(2)}, u32[]{:S(2)}) collective-permute-start(s32[512]{0:T(512)S(1)} %get-tuple-element.428), channel_id=1, source_target_pairs={{0,4},{4,8},{8,12},{12,16},{16,20},{20,24},{24,28},{28,32},{32,36}... | collective-permute-start | bytes 6152 | tf_op jit(solution)/shard_map/while/body/eval_jaxpr/ppermute | solution.py:16
  249.4 10.4 %collective-permute-start.2 = (s32[512]{0:T(512)S(1)}, s32[512]{0:T(512)S(1)}, u32[]{:S(2)}, u32[]{:S(2)}) collective-permute-start(s32[512]{0:T(512)S(1)} %get-tuple-element.428), channel_id=1, source_target_pairs={{0,4},{4,8},{8,12},{12,16},{16,20},{20,24},{24,28},{28,32},{32,36}... | collective-permute-start | bytes 6152 | tf_op jit(solution)/shard_map/while/body/eval_jaxpr/ppermute | solution.py:16
  273.9 10.4 %collective-permute-start.2 = (s32[512]{0:T(512)S(1)}, s32[512]{0:T(512)S(1)}, u32[]{:S(2)}, u32[]{:S(2)}) collective-permute-start(s32[512]{0:T(512)S(1)} %get-tuple-element.428), channel_id=1, source_target_pairs={{0,4},{4,8},{8,12},{12,16},{16,20},{20,24},{24,28},{28,32},{32,36}... | collective-permute-start | bytes 6152 | tf_op jit(solution)/shard_map/while/body/eval_jaxpr/ppermute | solution.py:16
  280.2 10.1 %collective-permute-start = (bf16[512,512]{0,1:T(8,128)(2,1)S(1)}, bf16[512,512]{0,1:T(8,128)(2,1)S(1)}, u32[]{:S(2)}, u32[]{:S(2)}) collective-permute-start(bf16[512,512]{0,1:T(8,128)(2,1)S(1)} %get-tuple-element.426), channel_id=1, source_target_pairs={{0,4},{4,8},{8,12},{12,16},{16,20},{20,24},{24,28},{28,32},{32,36}... | collective-permute-start | bytes 1572872 | tf_op jit(solution)/shard_map/while/body/eval_jaxpr/ppermute | solution.py:16
  298.4 10.4 %collective-permute-start.2 = (s32[512]{0:T(512)S(1)}, s32[512]{0:T(512)S(1)}, u32[]{:S(2)}, u32[]{:S(2)}) collective-permute-start(s32[512]{0:T(512)S(1)} %get-tuple-element.428), channel_id=1, source_target_pairs={{0,4},{4,8},{8,12},{12,16},{16,20},{20,24},{24,28},{28,32},{32,36}... | collective-permute-start | bytes 6152 | tf_op jit(solution)/shard_map/while/body/eval_jaxpr/ppermute | solution.py:16
  304.7 10.1 %collective-permute-start = (bf16[512,512]{0,1:T(8,128)(2,1)S(1)}, bf16[512,512]{0,1:T(8,128)(2,1)S(1)}, u32[]{:S(2)}, u32[]{:S(2)}) collective-permute-start(bf16[512,512]{0,1:T(8,128)(2,1)S(1)} %get-tuple-element.426), channel_id=1, source_target_pairs={{0,4},{4,8},{8,12},{12,16},{16,20},{20,24},{24,28},{28,32},{32,36}... | collective-permute-start | bytes 1572872 | tf_op jit(solution)/shard_map/while/body/eval_jaxpr/ppermute | solution.py:16
  322.9 10.4 %collective-permute-start.2 = (s32[512]{0:T(512)S(1)}, s32[512]{0:T(512)S(1)}, u32[]{:S(2)}, u32[]{:S(2)}) collective-permute-start(s32[512]{0:T(512)S(1)} %get-tuple-element.428), channel_id=1, source_target_pairs={{0,4},{4,8},{8,12},{12,16},{16,20},{20,24},{24,28},{28,32},{32,36}... | collective-permute-start | bytes 6152 | tf_op jit(solution)/shard_map/while/body/eval_jaxpr/ppermute | solution.py:16
  329.2 10.1 %collective-permute-start = (bf16[512,512]{0,1:T(8,128)(2,1)S(1)}, bf16[512,512]{0,1:T(8,128)(2,1)S(1)}, u32[]{:S(2)}, u32[]{:S(2)}) collective-permute-start(bf16[512,512]{0,1:T(8,128)(2,1)S(1)} %get-tuple-element.426), channel_id=1, source_target_pairs={{0,4},{4,8},{8,12},{12,16},{16,20},{20,24},{24,28},{28,32},{32,36}... | collective-permute-start | bytes 1572872 | tf_op jit(solution)/shard_map/while/body/eval_jaxpr/ppermute | solution.py:16
  347.4 10.4 %collective-permute-start.2 = (s32[512]{0:T(512)S(1)}, s32[512]{0:T(512)S(1)}, u32[]{:S(2)}, u32[]{:S(2)}) collective-permute-start(s32[512]{0:T(512)S(1)} %get-tuple-element.428), channel_id=1, source_target_pairs={{0,4},{4,8},{8,12},{12,16},{16,20},{20,24},{24,28},{28,32},{32,36}... | collective-permute-start | bytes 6152 | tf_op jit(solution)/shard_map/while/body/eval_jaxpr/ppermute | solution.py:16
  353.7 10.1 %collective-permute-start = (bf16[512,512]{0,1:T(8,128)(2,1)S(1)}, bf16[512,512]{0,1:T(8,128)(2,1)S(1)}, u32[]{:S(2)}, u32[]{:S(2)}) collective-permute-start(bf16[512,512]{0,1:T(8,128)(2,1)S(1)} %get-tuple-element.426), channel_id=1, source_target_pairs={{0,4},{4,8},{8,12},{12,16},{16,20},{20,24},{24,28},{28,32},{32,36}... | collective-permute-start | bytes 1572872 | tf_op jit(solution)/shard_map/while/body/eval_jaxpr/ppermute | solution.py:16
  371.9 10.4 %collective-permute-start.2 = (s32[512]{0:T(512)S(1)}, s32[512]{0:T(512)S(1)}, u32[]{:S(2)}, u32[]{:S(2)}) collective-permute-start(s32[512]{0:T(512)S(1)} %get-tuple-element.428), channel_id=1, source_target_pairs={{0,4},{4,8},{8,12},{12,16},{16,20},{20,24},{24,28},{28,32},{32,36}... | collective-permute-start | bytes 6152 | tf_op jit(solution)/shard_map/while/body/eval_jaxpr/ppermute | solution.py:16
  378.2 10.1 %collective-permute-start = (bf16[512,512]{0,1:T(8,128)(2,1)S(1)}, bf16[512,512]{0,1:T(8,128)(2,1)S(1)}, u32[]{:S(2)}, u32[]{:S(2)}) collective-permute-start(bf16[512,512]{0,1:T(8,128)(2,1)S(1)} %get-tuple-element.426), channel_id=1, source_target_pairs={{0,4},{4,8},{8,12},{12,16},{16,20},{20,24},{24,28},{28,32},{32,36}... | collective-permute-start | bytes 1572872 | tf_op jit(solution)/shard_map/while/body/eval_jaxpr/ppermute | solution.py:16
  396.4 10.4 %collective-permute-start.2 = (s32[512]{0:T(512)S(1)}, s32[512]{0:T(512)S(1)}, u32[]{:S(2)}, u32[]{:S(2)}) collective-permute-start(s32[512]{0:T(512)S(1)} %get-tuple-element.428), channel_id=1, source_target_pairs={{0,4},{4,8},{8,12},{12,16},{16,20},{20,24},{24,28},{28,32},{32,36}... | collective-permute-start | bytes 6152 | tf_op jit(solution)/shard_map/while/body/eval_jaxpr/ppermute | solution.py:16
  420.9 12.0 %collective-permute-start.2 = (s32[512]{0:T(512)S(1)}, s32[512]{0:T(512)S(1)}, u32[]{:S(2)}, u32[]{:S(2)}) collective-permute-start(s32[512]{0:T(512)S(1)} %get-tuple-element.428), channel_id=1, source_target_pairs={{0,4},{4,8},{8,12},{12,16},{16,20},{20,24},{24,28},{28,32},{32,36}... | collective-permute-start | bytes 6152 | tf_op jit(solution)/shard_map/while/body/eval_jaxpr/ppermute | solution.py:16
  428.4 10.5 %collective-permute-start = (bf16[512,512]{0,1:T(8,128)(2,1)S(1)}, bf16[512,512]{0,1:T(8,128)(2,1)S(1)}, u32[]{:S(2)}, u32[]{:S(2)}) collective-permute-start(bf16[512,512]{0,1:T(8,128)(2,1)S(1)} %get-tuple-element.426), channel_id=1, source_target_pairs={{0,4},{4,8},{8,12},{12,16},{16,20},{20,24},{24,28},{28,32},{32,36}... | collective-permute-start | bytes 1572872 | tf_op jit(solution)/shard_map/while/body/eval_jaxpr/ppermute | solution.py:16
  446.9 17.8 %collective-permute-start.2 = (s32[512]{0:T(512)S(1)}, s32[512]{0:T(512)S(1)}, u32[]{:S(2)}, u32[]{:S(2)}) collective-permute-start(s32[512]{0:T(512)S(1)} %get-tuple-element.428), channel_id=1, source_target_pairs={{0,4},{4,8},{8,12},{12,16},{16,20},{20,24},{24,28},{28,32},{32,36}... | collective-permute-start | bytes 6152 | tf_op jit(solution)/shard_map/while/body/eval_jaxpr/ppermute | solution.py:16
  451.3 13.4 %collective-permute-start.1 = (s32[512]{0:T(512)S(1)}, s32[512]{0:T(512)S(1)}, u32[]{:S(2)}, u32[]{:S(2)}) collective-permute-start(s32[512]{0:T(512)S(1)} %get-tuple-element.427), channel_id=1, source_target_pairs={{0,4},{4,8},{8,12},{12,16},{16,20},{20,24},{24,28},{28,32},{32,36}... | collective-permute-start | bytes 6152 | tf_op jit(solution)/shard_map/while/body/eval_jaxpr/ppermute | solution.py:16
  460.3 10.5 %collective-permute-start = (bf16[512,512]{0,1:T(8,128)(2,1)S(1)}, bf16[512,512]{0,1:T(8,128)(2,1)S(1)}, u32[]{:S(2)}, u32[]{:S(2)}) collective-permute-start(bf16[512,512]{0,1:T(8,128)(2,1)S(1)} %get-tuple-element.426), channel_id=1, source_target_pairs={{0,4},{4,8},{8,12},{12,16},{16,20},{20,24},{24,28},{28,32},{32,36}... | collective-permute-start | bytes 1572872 | tf_op jit(solution)/shard_map/while/body/eval_jaxpr/ppermute | solution.py:16
  (39 other events, 1015.8 us)
Sparse Core Ops, SparseCore 0:
  482.6 141.5 reduce-scatter.1
